TPU v7x, 32 devices: a whole 2x2x4 slice. The times are simulated.
32 devices in a mesh: groups: 2 (over y), lon: 4 (over z), chan: 2 (over x), lat: 2 (over core).
Axes of the slice: x: 2, y: 2, z: 4, core: 2. Of those that a mesh axis runs over, the one named last changes fastest.
Arguments:
- inputs: bfloat16 [256, 64, 512], P('chan', ('groups', 'lat'), 'lon'), parts along dimension 1, may hold values from -6 to 6
- cotangent: bfloat16 [256, 64, 512], P('chan', ('groups', 'lat'), 'lon'), parts along dimension 1, may hold values from -6 to 6
- weight: bfloat16 [3, 3, 256, 256], P(None, None, 'chan'), may hold values from -0.125 to 0.125
- bias_vector: float32 [256], P('chan'), may hold values from -4 to 4
Outputs:
- input_grad: bfloat16 [256, 64, 512], P('chan', ('groups', 'lat'), 'lon'), parts along dimension 1
- weight_grad: float32 [6, 3, 256, 256], P('groups', None, 'chan'), parts along dimension 0
- bias_grad: float32 [512], P(('groups', 'chan')), parts along dimension 0
There are 2 independent parts, one for each index of `groups`. A program takes and returns all parts, laid end to end along the dimension named above; an argument that names none is the same for every part. Nothing has to cross between parts.
All inputs are finite; a program needn't handle non-finite values.
Results may differ from a plain program's by a relative error of at most 0.007.
Values may be sent and summed in bfloat16 or wider, within the bound.
No kernel may reach another device: no remote copies, remote signals or barrier semaphores. Data moves between devices by JAX's collectives and lax.ppermute only.
A program may use at most 64 MiB of HBM per device.

v0:
```python
import jax
import jax.numpy as jnp
from jax import lax
from jax.sharding import PartitionSpec as P


def padded_2(shard, sides, width):
    for axis, dim in sides:
        devices, length = (lax.axis_size(axis), shard.shape[dim])
        up = [(i, (i + 1) % devices) for i in range(devices)]
        down = [(j, i) for i, j in up]
        last = lax.slice_in_dim(shard, length - width, length, axis=dim)
        initial = lax.slice_in_dim(shard, 0, width, axis=dim)
        before = lax.ppermute(last, axis, up)
        after = lax.ppermute(initial, axis, down)
        shard = jnp.concatenate([before, shard, after], axis=dim)
    return shard


def gelu_slope(preact):
    normal_cdf = 0.5 * (1.0 + jax.scipy.special.erf(preact * 0.7071067811865476))
    density = jnp.exp(-0.5 * preact * preact) * 0.3989422804014327
    return normal_cdf + preact * density


def mask_rims(padded):
    lat_index = lax.axis_index("lat")
    band_count = lax.axis_size("lat")
    row_ids = jnp.arange(padded.shape[1])
    outside = (row_ids == 0) & (lat_index == 0) | (row_ids == padded.shape[1] - 1) & (
        lat_index == band_count - 1
    )
    return jnp.where(outside[None, :, None], jnp.zeros((), padded.dtype), padded)


def window_of(field, first_row, first_col, row_count, column_count):
    return field[
        :, first_row : first_row + row_count, first_col : first_col + column_count
    ].reshape(field.shape[0], -1)


def local(inputs, cotangent, weight, bias_vector):
    own_channels, row_count, column_count = inputs.shape
    input_pad = mask_rims(padded_2(inputs, (("lon", 2), ("lat", 1)), 1))
    input_all = lax.all_gather(input_pad, "chan", axis=0, tiled=True)
    preact = jnp.zeros((own_channels, row_count * column_count), jnp.float32)
    for tap_row in range(3):
        for tap_col in range(3):
            window = window_of(input_all, tap_row, tap_col, row_count, column_count)
            preact = preact + jnp.dot(
                weight[tap_row, tap_col], window, preferred_element_type=jnp.float32
            )
    preact = preact + bias_vector[:, None]
    upstream = cotangent.reshape(own_channels, -1).astype(jnp.float32)
    grad_pre = (upstream * gelu_slope(preact)).astype(jnp.bfloat16)
    bias_part = jnp.sum(grad_pre.astype(jnp.float32), axis=1)
    taps = []
    for tap_row in range(3):
        row_taps = []
        for tap_col in range(3):
            window = window_of(input_all, tap_row, tap_col, row_count, column_count)
            row_taps.append(
                lax.dot_general(
                    grad_pre, window, (((1,), (1,)), ((), ())), preferred_element_type=jnp.float32
                )
            )
        taps.append(jnp.stack(row_taps))
    weight_part = jnp.stack(taps)
    weight_grad, bias_grad = lax.psum((weight_part, bias_part), ("lon", "lat"))
    grad_field = grad_pre.reshape(own_channels, row_count, column_count)
    grad_pad = mask_rims(padded_2(grad_field, (("lon", 2), ("lat", 1)), 1))
    amount = lax.axis_size("chan") * own_channels
    summed = jnp.zeros((amount, row_count * column_count), jnp.float32)
    for tap_row in range(3):
        for tap_col in range(3):
            kernel_cols = weight[tap_row, tap_col]
            window = window_of(grad_pad, 2 - tap_row, 2 - tap_col, row_count, column_count)
            summed = summed + lax.dot_general(
                kernel_cols, window, (((0,), (0,)), ((), ())), preferred_element_type=jnp.float32
            )
    input_sum = lax.psum_scatter(
        summed.reshape(amount, row_count, column_count), "chan", scatter_dimension=0, tiled=True
    )
    return (input_sum.astype(jnp.bfloat16), weight_grad, bias_grad)


def solution(mesh):
    placed = (
        P("chan", ("groups", "lat"), "lon"),
        P("chan", ("groups", "lat"), "lon"),
        P(None, None, "chan", None),
        P("chan"),
    )
    return jax.shard_map(
        local,
        mesh=mesh,
        in_specs=placed,
        out_specs=(
            P("chan", ("groups", "lat"), "lon"),
            P("groups", None, "chan", None),
            P(("groups", "chan")),
        ),
        check_vma=False,
    )
```

profile of v0, /device:TPU:0, one launch (start us, length us, event | category | flops | bytes accessed | tf_op | source)
XLA Modules:
  0.0 177.4 jit_solution(9235394544272731963)
XLA Ops:
  7.2 1.5 copy.13
  8.8 3.1 %collective-permute-start = (bf16[128,16,1]{0,2,1:T(2,128)(2,1)S(1)}, bf16[128,16,1]{0,2,1:T(2,128)(2,1)S(1)}, u32[]{:S(2)}, u32[]{:S(2)}) collective-permute-start(bf16[128,16,1]{0,2,1:T(2,128)(2,1)S(1)} %get-tuple-element.27), channel_id=1, source_target_pairs={{0,4},{4,8},{8,12},{12,0},{1,5},{5,9},{9,13},{13,1},{2,6},{6,10},{... | collective-permute-start | bytes 12296 | tf_op jit(solution)/shard_map/ppermute | solution.py:14
  11.8 2.1 %collective-permute-start.1 = (bf16[128,16,1]{0,2,1:T(2,128)(2,1)S(1)}, bf16[128,16,1]{0,2,1:T(2,128)(2,1)S(1)}, u32[]{:S(2)}, u32[]{:S(2)}) collective-permute-start(bf16[128,16,1]{0,2,1:T(2,128)(2,1)S(1)} %get-tuple-element.28), channel_id=1, source_target_pairs={{4,0},{8,4},{12,8},{0,12},{5,1},{9,5},{13,9},{1,13},{6,2},{10,6},{... | collective-permute-start | bytes 12296 | tf_op jit(solution)/shard_map/ppermute | solution.py:15
  13.9 1.6 collective-permute-done
  15.7 0.5 collective-permute-start.3
  16.2 0.7 collective-permute-done.2
  17.0 1.1 maximum_select_fusion
  18.2 1.4 copy.12
  19.6 23.9 %all-gather.2.cloned.1.call-done = bf16[256,18,130]{0,2,1:T(8,128)(2,1)} async-done(((bf16[128,18,130]{0,2,1:T(8,128)(2,1)}), bf16[256,18,130]{0,2,1:T(8,128)(2,1)}) %all-gather.2.cloned.1.call-update) | async-done | bytes 1198096 | tf_op jit(solution)/shard_map/all_gather | solution.py:45
  43.5 8.3 %fusion.46 = (bf16[256,16,128]{0,2,1:T(8,128)(2,1)S(1)}, bf16[256,16,128]{0,2,1:T(8,128)(2,1)S(1)}, bf16[256,16,128]{0,2,1:T(8,128)(2,1)S(1)}, bf16[256,16,128]{...) fusion(bf16[256,18,130]{0,2,1:T(8,128)(2,1)} %all-gather.2.clon, ...), kind=kLoop, calls=%fused_computation.86 | loop fusion | bytes 18874368 | tf_op jit(solution)/shard_map/slice | solution.py:37
  51.9 0.4 fusion.26
  52.3 0.4 convolution_add_fusion.15
  52.9 0.4 convolution_add_fusion.14
  53.3 0.4 convolution_add_fusion.13
  53.7 0.4 convolution_add_fusion.12
  54.2 0.4 convolution_add_fusion.11
  54.6 0.4 convolution_add_fusion.10
  55.1 0.4 convolution_add_fusion.9
  55.6 0.7 copy-done.13
  56.3 0.7 convert_reduce_fusion
  57.1 1.5 collective-permute-start.4
  58.6 2.3 %collective-permute-start.5 = (bf16[128,16,1]{0,2,1:T(2,128)(2,1)S(1)}, bf16[128,16,1]{0,2,1:T(2,128)(2,1)S(1)}, u32[]{:S(2)}, u32[]{:S(2)}) collective-permute-start(bf16[128,16,1]{0,2,1:T(2,128)(2,1)S(1)} %get-tuple-element.26), channel_id=1, source_target_pairs={{4,0},{8,4},{12,8},{0,12},{5,1},{9,5},{13,9},{1,13},{6,2},{10,6},{... | collective-permute-start | bytes 12296 | tf_op jit(solution)/shard_map/ppermute | solution.py:15
  60.9 1.6 collective-permute-done.4
  62.7 0.5 collective-permute-start.7
  63.2 0.7 collective-permute-done.6
  64.4 0.9 fusion.47
  65.3 0.4 fusion.24
  65.7 0.4 convolution_add_fusion.7
  66.1 0.4 convolution_add_fusion.6
  66.6 0.4 convolution_add_fusion.5
  67.0 0.4 convolution_add_fusion.4
  67.4 0.4 convolution_add_fusion.3
  67.8 0.4 convolution_add_fusion.2
  68.2 0.4 convolution_add_fusion.1
  68.6 1.7 convolution_add_fusion
  70.4 3.0 %copy.16 = f32[256,16,128]{2,1,0:T(8,128)} copy(f32[256,16,128]{0,2,1:T(8,128)} %bitcast.154) | data formatting | bytes 4194304 | tf_op jit(solution)/shard_map/reshape | solution.py:82
  73.6 1.7 convolution_bitcast_fusion
  75.3 1.7 convolution_bitcast_fusion.1
  77.0 0.4 convolution_bitcast_fusion.2
  77.4 0.4 convolution_bitcast_fusion.3
  77.8 0.4 copy-done.5
  79.0 0.5 copy-done.1
  80.6 1.1 pad_maximum_fusion
  81.8 17.9 %psum.15 = f32[128]{0:T(128)} all-reduce(f32[128]{0:T(128)S(1)} %get-tuple-element.29), channel_id=1, replica_groups=mesh['groups'=2,'lon'=4,'chan'=2,'lat'=2] {'lon','lat'}, use_global_device_ids=true, to_apply=%region_3.4 | all-reduce | flops 128 | bytes 1024 | tf_op jit(solution)/shard_map/psum | solution.py:69
  99.6 6.3 %reduce-scatter.2.cloned.1.call-done = f32[128,16,128]{2,1,0:T(8,128)} async-done(((f32[256,16,128]{2,1,0:T(8,128)}), f32[128,16,128]{2,1,0:T(8,128)}) %reduce-scatter.2.cloned.1.call-update) | async-done | bytes 1048592 | tf_op jit(solution)/shard_map/reduce_scatter | solution.py:81
  105.9 2.1 %convert_element_type.18 = bf16[128,16,128]{2,1,0:T(8,128)(2,1)} convert(f32[128,16,128]{2,1,0:T(8,128)} %reduce-scatter.2.cloned.1.call-done) | non-fusion elementwise | flops 262144 | bytes 1572864 | tf_op jit(solution)/shard_map/convert_element_type | solution.py:84
  108.0 60.5 %all-reduce.2.cloned.1.call-done = f32[3,3,128,256]{3,2,1,0:T(8,128)} async-done(((f32[3,3,128,256]{3,2,1,0:T(8,128)}), f32[3,3,128,256]{3,2,1,0:T(8,128)}) %all-reduce.2.cloned.1.call-update) | async-done | bytes 1179664 | tf_op jit(solution)/shard_map/psum | solution.py:69
  168.5 2.4 %copy.18 = f32[3,3,128,256]{3,2,1,0:T(8,128)} copy(f32[3,3,128,256]{3,2,1,0:T(8,128)} %all-reduce.2.cloned.1.call-done) | data formatting | bytes 2359296
  (54 shorter events, 3.3 us)
Async XLA Ops:
  7.2 11.1 %copy-start.14 = (bf16[128,16,128]{2,1,0:T(8,128)(2,1)S(1)}, bf16[128,16,128]{2,1,0:T(8,128)(2,1)}, u32[]{:S(2)}) copy-start(bf16[128,16,128]{2,1,0:T(8,128)(2,1)} %param.5) | copy-start | bytes 1572868
  7.2 36.3 %all-gather.2.cloned.1.call-start = ((), (), s32[]{:S(2)}) async-start(), calls=%async_computation.1 | async-start | bytes 1880064 | tf_op jit(solution)/shard_map/all_gather | solution.py:45
  8.8 6.8 %collective-permute-start = (bf16[128,16,1]{0,2,1:T(2,128)(2,1)S(1)}, bf16[128,16,1]{0,2,1:T(2,128)(2,1)S(1)}, u32[]{:S(2)}, u32[]{:S(2)}) collective-permute-start(bf16[128,16,1]{0,2,1:T(2,128)(2,1)S(1)} %get-tuple-element.27), channel_id=1, source_target_pairs={{0,4},{4,8},{8,12},{12,0},{1,5},{5,9},{9,13},{13,1},{2,6},{6,10},{... | collective-permute-start | bytes 12296 | tf_op jit(solution)/shard_map/ppermute | solution.py:14
  11.8 3.7 %collective-permute-start.1 = (bf16[128,16,1]{0,2,1:T(2,128)(2,1)S(1)}, bf16[128,16,1]{0,2,1:T(2,128)(2,1)S(1)}, u32[]{:S(2)}, u32[]{:S(2)}) collective-permute-start(bf16[128,16,1]{0,2,1:T(2,128)(2,1)S(1)} %get-tuple-element.28), channel_id=1, source_target_pairs={{4,0},{8,4},{12,8},{0,12},{5,1},{9,5},{13,9},{1,13},{6,2},{10,6},{... | collective-permute-start | bytes 12296 | tf_op jit(solution)/shard_map/ppermute | solution.py:15
  15.6 1.3 collective-permute-start.2
  15.7 1.4 collective-permute-start.3
  18.2 87.8 %reduce-scatter.2.cloned.1.call-start = ((), (), s32[]{:S(2)}) async-start(), calls=%async_computation.2 | async-start | bytes 3145728 | tf_op jit(solution)/shard_map/reduce_scatter | solution.py:81
  19.6 32.3 %copy-start.12 = (bf16[3,3,128,256]{3,2,1,0:T(8,128)(2,1)S(1)}, bf16[3,3,128,256]{3,2,1,0:T(8,128)(2,1)}, u32[]{:S(2)}) copy-start(bf16[3,3,128,256]{3,2,1,0:T(8,128)(2,1)} %param.6) | copy-start | bytes 1769476
  51.8 1.0 copy-start
  51.9 1.4 copy-start.2
  51.9 1.9 %copy-start.4 = (bf16[256,16,128]{0,2,1:T(8,128)(2,1)}, bf16[256,16,128]{0,2,1:T(8,128)(2,1)S(1)}, u32[]{:S(2)}) copy-start(bf16[256,16,128]{0,2,1:T(8,128)(2,1)S(1)} %get-tuple-element.7) | copy-start | bytes 3145732
  51.9 2.3 %copy-start.6 = (bf16[256,16,128]{0,2,1:T(8,128)(2,1)}, bf16[256,16,128]{0,2,1:T(8,128)(2,1)S(1)}, u32[]{:S(2)}) copy-start(bf16[256,16,128]{0,2,1:T(8,128)(2,1)S(1)} %get-tuple-element.6) | copy-start | bytes 3145732
  51.9 2.7 %copy-start.8 = (bf16[256,16,128]{0,2,1:T(8,128)(2,1)}, bf16[256,16,128]{0,2,1:T(8,128)(2,1)S(1)}, u32[]{:S(2)}) copy-start(bf16[256,16,128]{0,2,1:T(8,128)(2,1)S(1)} %get-tuple-element.5) | copy-start | bytes 3145732
  51.9 3.2 %copy-start.10 = (bf16[256,16,128]{0,2,1:T(8,128)(2,1)}, bf16[256,16,128]{0,2,1:T(8,128)(2,1)S(1)}, u32[]{:S(2)}) copy-start(bf16[256,16,128]{0,2,1:T(8,128)(2,1)S(1)} %get-tuple-element.4) | copy-start | bytes 3145732
  51.9 3.6 %copy-start.11 = (bf16[256,16,128]{0,2,1:T(8,128)(2,1)}, bf16[256,16,128]{0,2,1:T(8,128)(2,1)S(1)}, u32[]{:S(2)}) copy-start(bf16[256,16,128]{0,2,1:T(8,128)(2,1)S(1)} %get-tuple-element.3) | copy-start | bytes 3145732
  55.1 1.2 copy-start.13
  55.1 1.2 copy-start.15
  57.1 5.5 %collective-permute-start.4 = (bf16[128,16,1]{0,2,1:T(2,128)(2,1)S(1)}, bf16[128,16,1]{0,2,1:T(2,128)(2,1)S(1)}, u32[]{:S(2)}, u32[]{:S(2)}) collective-permute-start(bf16[128,16,1]{0,2,1:T(2,128)(2,1)S(1)} %get-tuple-element.25), channel_id=1, source_target_pairs={{0,4},{4,8},{8,12},{12,0},{1,5},{5,9},{9,13},{13,1},{2,6},{6,10},{... | collective-permute-start | bytes 12296 | tf_op jit(solution)/shard_map/ppermute | solution.py:14
  58.6 4.0 %collective-permute-start.5 = (bf16[128,16,1]{0,2,1:T(2,128)(2,1)S(1)}, bf16[128,16,1]{0,2,1:T(2,128)(2,1)S(1)}, u32[]{:S(2)}, u32[]{:S(2)}) collective-permute-start(bf16[128,16,1]{0,2,1:T(2,128)(2,1)S(1)} %get-tuple-element.26), channel_id=1, source_target_pairs={{4,0},{8,4},{12,8},{0,12},{5,1},{9,5},{13,9},{1,13},{6,2},{10,6},{... | collective-permute-start | bytes 12296 | tf_op jit(solution)/shard_map/ppermute | solution.py:15
  62.6 1.3 collective-permute-start.6
  62.7 1.4 collective-permute-start.7
  73.4 95.1 %all-reduce.2.cloned.1.call-start = ((), (), s32[]{:S(2)}) async-start(), calls=%async_computation.3 | async-start | bytes 2359296 | tf_op jit(solution)/shard_map/psum | solution.py:69
  73.6 3.3 %copy-start.9 = (bf16[256,16,128]{0,2,1:T(8,128)(2,1)S(1)}, bf16[256,16,128]{0,2,1:T(8,128)(2,1)}, u32[]{:S(2)}) copy-start(bf16[256,16,128]{0,2,1:T(8,128)(2,1)} %copy-done.8) | copy-start | bytes 3145732
  75.3 2.1 %copy-start.7 = (bf16[256,16,128]{0,2,1:T(8,128)(2,1)S(1)}, bf16[256,16,128]{0,2,1:T(8,128)(2,1)}, u32[]{:S(2)}) copy-start(bf16[256,16,128]{0,2,1:T(8,128)(2,1)} %copy-done.6) | copy-start | bytes 3145732
  77.0 1.2 copy-start.5
  77.4 1.3 copy-start.3
  78.2 1.3 copy-start.1
Sparse Core Ops, SparseCore 0:
  18.3 25.1 all-gather.1
  73.5 32.3 reduce-scatter.1
  109.0 59.5 all-reduce.1
where the time goes:
time: 178 us; the launch traced here: 177 us
  waiting for transfers between devices  95.8 us (54%)
  local copies, waits for them, and re-layouts  19.5 us (11%)
  blocking collectives  17.9 us (10%)
  matrix products  15 us (8%)
  between operations  14.2 us (8%)
  starting transfers between devices  10.5 us (6%)
  other arithmetic  4.73 us (3%)
    psum x1, waiting for transfers between devices, local(): weight_grad, bias_grad = lax.psum((weight_part, bias_part), ('lon', 'lat'))  60.5 us
    all_gather x1, waiting for transfers between devices, local(): input_all = lax.all_gather(input_pad, 'chan', axis=0, tiled=True)  23.9 us
    psum x1, blocking collectives, local(): weight_grad, bias_grad = lax.psum((weight_part, bias_part), ('lon', 'lat'))  17.9 us
    slice x2, local copies, waits for them, and re-layouts, window_of(): field[:, first_row:first_row + row_count, first_col:first_col + column_co...  9.24 us
    reduce_scatter x1, waiting for transfers between devices, local(): lax.psum_scatter(summed.reshape(amount, row_count, column_count), 'chan',...  6.31 us
    unnamed x34, local copies, waits for them, and re-layouts  5.76 us
    dot_general x9, matrix products, local(): lax.dot_general(grad_pre, window, (((1,), (1,)), ((), ())), preferred_ele...  5.76 us
    ppermute x4, starting transfers between devices, padded_2(): after = lax.ppermute(initial, axis, down)  5.42 us
  transfers between devices with their start and end apart: 11, of which 9 were waited for; matrix products, arithmetic and copies ran while one was open for 6% of the time, Pallas kernels for 0%

commit v1 on v0

--- a/solution.py
+++ b/solution.py
@@ -66,7 +66,7 @@
             )
         taps.append(jnp.stack(row_taps))
     weight_part = jnp.stack(taps)
-    weight_grad, bias_grad = lax.psum((weight_part, bias_part), ("lon", "lat"))
+    weight_grad, bias_grad = lax.psum(lax.psum((weight_part, bias_part), "lat"), "lon")
     grad_field = grad_pre.reshape(own_channels, row_count, column_count)
     grad_pad = mask_rims(padded_2(grad_field, (("lon", 2), ("lat", 1)), 1))
     amount = lax.axis_size("chan") * own_channels

time: 178 us -> 190 us (1.067)
  waiting for transfers between devices: 95.8 us -> 119 us
  matrix products: 15 us -> 11.1 us
  local copies, waits for them, and re-layouts: 19.5 us -> 15.8 us
  blocking collectives: 17.9 us -> 14.9 us
    reduce_scatter x1, waiting for transfers between devices: 6.31 us -> 20.5 us  [local(): lax.psum_scatter(summed.reshape(amount, row_count, column_count), 'chan',...]
    psum x1 -> x2, waiting for transfers between devices: 60.5 us -> 69.1 us  [the longest x1 56.1 us: local(): lax.psum(lax.psum((weight_part, bias_part), 'lat'), 'lon')]
    psum x1 -> x2, blocking collectives: 17.9 us -> 14.9 us  [the longest x1 12.4 us: local(): lax.psum(lax.psum((weight_part, bias_part), 'lat'), 'lon')]
    dot_general x9, matrix products: 5.76 us -> 3.19 us  [local(): lax.dot_general(grad_pre, window, (((1,), (1,)), ((), ())), preferred_ele...]
    unnamed x34 -> x8, local copies, waits for them, and re-layouts: 5.76 us -> 4.1 us
  transfers between devices with their start and end apart: 11 -> 12, of which waited for: 9 -> 8; matrix products, arithmetic and copies ran while one was open for 6% -> 6% of each run, Pallas kernels for 0% -> 0%
where the time goes in v1:
time: 190 us
  waiting for transfers between devices  119 us (63%)
  local copies, waits for them, and re-layouts  15.8 us (8%)
  blocking collectives  14.9 us (8%)
  between operations  14.1 us (7%)
  matrix products  11.1 us (6%)
  starting transfers between devices  10.5 us (6%)
  other arithmetic  4.7 us (2%)
    psum x1, waiting for transfers between devices, local(): lax.psum(lax.psum((weight_part, bias_part), 'lat'), 'lon')  56.1 us
    all_gather x1, waiting for transfers between devices, local(): input_all = lax.all_gather(input_pad, 'chan', axis=0, tiled=True)  24.8 us
    reduce_scatter x1, waiting for transfers between devices, local(): lax.psum_scatter(summed.reshape(amount, row_count, column_count), 'chan',...  20.5 us
    psum x1, waiting for transfers between devices, local(): lax.psum((weight_part, bias_part), 'lat')  13.1 us
    psum x1, blocking collectives, local(): lax.psum(lax.psum((weight_part, bias_part), 'lat'), 'lon')  12.4 us
    slice x2, local copies, waits for them, and re-layouts, window_of(): field[:, first_row:first_row + row_count, first_col:first_col + column_co...  9.2 us
    ppermute x4, starting transfers between devices, padded_2(): after = lax.ppermute(initial, axis, down)  5.41 us
    ppermute x4, starting transfers between devices, padded_2(): before = lax.ppermute(last, axis, up)  4.77 us
  transfers between devices with their start and end apart: 12, of which 8 were waited for; matrix products, arithmetic and copies ran while one was open for 6% of the time, Pallas kernels for 0%

profile of v1, /device:TPU:0, one launch (start us, length us, event | category | flops | bytes accessed | tf_op | source)
XLA Modules:
  0.0 189.7 jit_solution(6016607692126858154)
XLA Ops:
  7.2 1.5 copy.13
  8.8 3.1 %collective-permute-start = (bf16[128,16,1]{0,2,1:T(2,128)(2,1)S(1)}, bf16[128,16,1]{0,2,1:T(2,128)(2,1)S(1)}, u32[]{:S(2)}, u32[]{:S(2)}) collective-permute-start(bf16[128,16,1]{0,2,1:T(2,128)(2,1)S(1)} %get-tuple-element.27), channel_id=1, source_target_pairs={{0,4},{4,8},{8,12},{12,0},{1,5},{5,9},{9,13},{13,1},{2,6},{6,10},{... | collective-permute-start | bytes 12296 | tf_op jit(solution)/shard_map/ppermute | solution.py:14
  11.8 2.1 %collective-permute-start.1 = (bf16[128,16,1]{0,2,1:T(2,128)(2,1)S(1)}, bf16[128,16,1]{0,2,1:T(2,128)(2,1)S(1)}, u32[]{:S(2)}, u32[]{:S(2)}) collective-permute-start(bf16[128,16,1]{0,2,1:T(2,128)(2,1)S(1)} %get-tuple-element.28), channel_id=1, source_target_pairs={{4,0},{8,4},{12,8},{0,12},{5,1},{9,5},{13,9},{1,13},{6,2},{10,6},{... | collective-permute-start | bytes 12296 | tf_op jit(solution)/shard_map/ppermute | solution.py:15
  13.9 1.6 collective-permute-done
  15.7 0.5 collective-permute-start.3
  16.2 0.7 collective-permute-done.2
  17.0 1.1 maximum_select_fusion
  18.2 0.4 copy.12
  18.7 24.8 %all-gather.2.cloned.1.call-done = bf16[256,18,130]{0,2,1:T(8,128)(2,1)} async-done(((bf16[128,18,130]{0,2,1:T(8,128)(2,1)}), bf16[256,18,130]{0,2,1:T(8,128)(2,1)}) %all-gather.2.cloned.1.call-update) | async-done | bytes 1198096 | tf_op jit(solution)/shard_map/all_gather | solution.py:45
  43.5 8.3 %fusion.46 = (bf16[256,16,128]{0,2,1:T(8,128)(2,1)S(1)}, bf16[256,16,128]{0,2,1:T(8,128)(2,1)S(1)}, bf16[256,16,128]{0,2,1:T(8,128)(2,1)S(1)}, bf16[256,16,128]{...) fusion(bf16[256,18,130]{0,2,1:T(8,128)(2,1)} %all-gather.2.clon, ...), kind=kLoop, calls=%fused_computation.86 | loop fusion | bytes 18874368 | tf_op jit(solution)/shard_map/slice | solution.py:37
  51.8 0.4 fusion.26
  52.2 0.4 convolution_add_fusion.15
  52.6 0.4 convolution_add_fusion.14
  53.1 0.4 convolution_add_fusion.13
  53.5 0.4 convolution_add_fusion.12
  54.0 0.4 convolution_add_fusion.11
  54.4 0.4 convolution_add_fusion.10
  54.8 0.4 convolution_add_fusion.9
  55.5 0.7 convert_reduce_fusion
  56.2 0.4 convolution_bitcast_fusion
  56.6 0.4 convolution_bitcast_fusion.1
  57.0 0.4 convolution_bitcast_fusion.2
  57.3 0.4 convolution_bitcast_fusion.3
  57.7 0.4 convolution_bitcast_fusion.4
  58.0 0.4 convolution_bitcast_fusion.5
  59.5 1.6 collective-permute-start.4
  61.1 2.3 %collective-permute-start.5 = (bf16[128,16,1]{0,2,1:T(2,128)(2,1)S(1)}, bf16[128,16,1]{0,2,1:T(2,128)(2,1)S(1)}, u32[]{:S(2)}, u32[]{:S(2)}) collective-permute-start(bf16[128,16,1]{0,2,1:T(2,128)(2,1)S(1)} %get-tuple-element.26), channel_id=1, source_target_pairs={{4,0},{8,4},{12,8},{0,12},{5,1},{9,5},{13,9},{1,13},{6,2},{10,6},{... | collective-permute-start | bytes 12296 | tf_op jit(solution)/shard_map/ppermute | solution.py:15
  63.5 1.5 collective-permute-done.4
  65.1 0.5 collective-permute-start.7
  65.6 1.1 pad_maximum_fusion
  67.3 0.9 fusion.47
  68.2 0.4 fusion.24
  68.7 0.4 convolution_add_fusion.7
  69.1 0.4 convolution_add_fusion.6
  69.5 0.4 convolution_add_fusion.5
  69.9 0.4 convolution_add_fusion.4
  70.4 0.4 convolution_add_fusion.3
  70.8 0.4 convolution_add_fusion.2
  71.2 0.4 convolution_add_fusion.1
  71.6 0.4 convolution_add_fusion
  72.1 2.0 %copy.16 = f32[256,16,128]{2,1,0:T(8,128)} copy(f32[256,16,128]{0,2,1:T(8,128)S(1)} %bitcast.154) | data formatting | bytes 4194304 | tf_op jit(solution)/shard_map/reshape | solution.py:82
  74.1 13.1 %all-reduce.3.cloned.1.call-done = f32[3,3,128,256]{3,2,1,0:T(8,128)} async-done(((f32[3,3,128,256]{3,2,1,0:T(8,128)}), f32[3,3,128,256]{3,2,1,0:T(8,128)}) %all-reduce.3.cloned.1.call-update) | async-done | bytes 1179664 | tf_op jit(solution)/shard_map/psum | solution.py:69
  87.2 2.5 %psum.30 = f32[128]{0:T(128)S(1)} all-reduce(f32[128]{0:T(128)S(1)} %get-tuple-element.29), channel_id=1, replica_groups=mesh['groups'=2,'lon'=4,'chan'=2,'lat'=2] {'lat'}, use_global_device_ids=true, to_apply=%region_4.5 | all-reduce | flops 128 | bytes 1024 | tf_op jit(solution)/shard_map/psum | solution.py:69
  89.7 12.4 %psum.31 = f32[128]{0:T(128)} all-reduce(f32[128]{0:T(128)S(1)} %psum.30), channel_id=1, replica_groups=mesh['groups'=2,'lon'=4,'chan'=2,'lat'=2] {'lon'}, use_global_device_ids=true, to_apply=%region_5.6 | all-reduce | flops 128 | bytes 1024 | tf_op jit(solution)/shard_map/psum | solution.py:69
  102.1 20.5 %reduce-scatter.2.cloned.1.call-done = f32[128,16,128]{2,1,0:T(8,128)} async-done(((f32[256,16,128]{2,1,0:T(8,128)}), f32[128,16,128]{2,1,0:T(8,128)}) %reduce-scatter.2.cloned.1.call-update) | async-done | bytes 1048592 | tf_op jit(solution)/shard_map/reduce_scatter | solution.py:81
  122.6 2.1 %convert_element_type.18 = bf16[128,16,128]{2,1,0:T(8,128)(2,1)} convert(f32[128,16,128]{2,1,0:T(8,128)} %reduce-scatter.2.cloned.1.call-done) | non-fusion elementwise | flops 262144 | bytes 1572864 | tf_op jit(solution)/shard_map/convert_element_type | solution.py:84
  124.7 56.1 %all-reduce.5.cloned.1.call-done = f32[3,3,128,256]{3,2,1,0:T(8,128)} async-done(((f32[3,3,128,256]{3,2,1,0:T(8,128)}), f32[3,3,128,256]{3,2,1,0:T(8,128)}) %all-reduce.5.cloned.1.call-update) | async-done | bytes 1179664 | tf_op jit(solution)/shard_map/psum | solution.py:69
  180.8 2.4 %copy.19 = f32[3,3,128,256]{3,2,1,0:T(8,128)} copy(f32[3,3,128,256]{3,2,1,0:T(8,128)} %all-reduce.5.cloned.1.call-done) | data formatting | bytes 2359296
  (32 shorter events, 2.5 us)
Async XLA Ops:
  7.2 11.0 %copy-start.1 = (bf16[128,16,128]{2,1,0:T(8,128)(2,1)S(1)}, bf16[128,16,128]{2,1,0:T(8,128)(2,1)}, u32[]{:S(2)}) copy-start(bf16[128,16,128]{2,1,0:T(8,128)(2,1)} %param.5) | copy-start | bytes 1572868
  7.2 36.3 %all-gather.2.cloned.1.call-start = ((), (), s32[]{:S(2)}) async-start(), calls=%async_computation.1 | async-start | bytes 1880064 | tf_op jit(solution)/shard_map/all_gather | solution.py:45
  8.8 6.8 %collective-permute-start = (bf16[128,16,1]{0,2,1:T(2,128)(2,1)S(1)}, bf16[128,16,1]{0,2,1:T(2,128)(2,1)S(1)}, u32[]{:S(2)}, u32[]{:S(2)}) collective-permute-start(bf16[128,16,1]{0,2,1:T(2,128)(2,1)S(1)} %get-tuple-element.27), channel_id=1, source_target_pairs={{0,4},{4,8},{8,12},{12,0},{1,5},{5,9},{9,13},{13,1},{2,6},{6,10},{... | collective-permute-start | bytes 12296 | tf_op jit(solution)/shard_map/ppermute | solution.py:14
  11.8 3.7 %collective-permute-start.1 = (bf16[128,16,1]{0,2,1:T(2,128)(2,1)S(1)}, bf16[128,16,1]{0,2,1:T(2,128)(2,1)S(1)}, u32[]{:S(2)}, u32[]{:S(2)}) collective-permute-start(bf16[128,16,1]{0,2,1:T(2,128)(2,1)S(1)} %get-tuple-element.28), channel_id=1, source_target_pairs={{4,0},{8,4},{12,8},{0,12},{5,1},{9,5},{13,9},{1,13},{6,2},{10,6},{... | collective-permute-start | bytes 12296 | tf_op jit(solution)/shard_map/ppermute | solution.py:15
  15.6 1.3 collective-permute-start.2
  15.7 1.4 collective-permute-start.3
  18.1 69.1 %all-reduce.3.cloned.1.call-start = ((), (), s32[]{:S(2)}) async-start(), calls=%async_computation.3 | async-start | bytes 2359296 | tf_op jit(solution)/shard_map/psum | solution.py:69
  18.6 33.1 %copy-start = (bf16[3,3,128,256]{3,2,1,0:T(8,128)(2,1)S(1)}, bf16[3,3,128,256]{3,2,1,0:T(8,128)(2,1)}, u32[]{:S(2)}) copy-start(bf16[3,3,128,256]{3,2,1,0:T(8,128)(2,1)} %param.6) | copy-start | bytes 1769476
  54.8 0.7 copy-start.2
  59.5 5.5 %collective-permute-start.4 = (bf16[128,16,1]{0,2,1:T(2,128)(2,1)S(1)}, bf16[128,16,1]{0,2,1:T(2,128)(2,1)S(1)}, u32[]{:S(2)}, u32[]{:S(2)}) collective-permute-start(bf16[128,16,1]{0,2,1:T(2,128)(2,1)S(1)} %get-tuple-element.25), channel_id=1, source_target_pairs={{0,4},{4,8},{8,12},{12,0},{1,5},{5,9},{9,13},{13,1},{2,6},{6,10},{... | collective-permute-start | bytes 12296 | tf_op jit(solution)/shard_map/ppermute | solution.py:14
  61.1 4.0 %collective-permute-start.5 = (bf16[128,16,1]{0,2,1:T(2,128)(2,1)S(1)}, bf16[128,16,1]{0,2,1:T(2,128)(2,1)S(1)}, u32[]{:S(2)}, u32[]{:S(2)}) collective-permute-start(bf16[128,16,1]{0,2,1:T(2,128)(2,1)S(1)} %get-tuple-element.26), channel_id=1, source_target_pairs={{4,0},{8,4},{12,8},{0,12},{5,1},{9,5},{13,9},{1,13},{6,2},{10,6},{... | collective-permute-start | bytes 12296 | tf_op jit(solution)/shard_map/ppermute | solution.py:15
  65.1 1.9 %collective-permute-start.6 = (bf16[128,1,130]{0,2,1:T(8,128)(2,1)S(1)}, bf16[128,1,130]{0,2,1:T(8,128)(2,1)S(1)}, u32[]{:S(2)}, u32[]{:S(2)}) collective-permute-start(bf16[128,1,130]{0,2,1:T(8,128)(2,1)S(1)} %get-tuple-element.21), channel_id=1, source_target_pairs={{0,1},{1,0},{2,3},{3,2},{4,5},{5,4},{6,7},{7,6},{8,9},{9,8},{10,11... | collective-permute-start | bytes 99848 | tf_op jit(solution)/shard_map/ppermute | solution.py:14
  65.1 1.9 collective-permute-start.7
  66.7 55.9 %reduce-scatter.2.cloned.1.call-start = ((), (), s32[]{:S(2)}) async-start(), calls=%async_computation.2 | async-start | bytes 3145728 | tf_op jit(solution)/shard_map/reduce_scatter | solution.py:81
  74.1 106.7 %all-reduce.5.cloned.1.call-start = ((), (), s32[]{:S(2)}) async-start(), calls=%async_computation.4 | async-start | bytes 2359296 | tf_op jit(solution)/shard_map/psum | solution.py:69
Sparse Core Ops, SparseCore 0:
  18.3 25.1 all-gather.1
  66.9 20.3 all-reduce.2
  89.6 33.0 reduce-scatter.1
  124.8 55.8 all-reduce.4
